TPU v7x, 512 devices: a whole 4x8x8 slice. The times are simulated.
512 devices in a mesh: tm: 32 (over y, x), rows: 16 (over z, core).
Axes of the slice: x: 4, y: 8, z: 8, core: 2. Of those that a mesh axis runs over, the one named last changes fastest.
Arguments:
- features: bfloat16 [64, 16, 40, 384], P('tm', 'rows'), may hold values from -6 to 6
- gain_one: float32 [384], replicated, may hold values from 0.1 to 1.9
- weight_one: bfloat16 [384, 3, 3, 3, 384], P('rows'), may hold values from -0.0625 to 0.0625
- bias_one: float32 [384], replicated, may hold values from -3 to 3
- gain_two: float32 [384], replicated, may hold values from 0.1 to 1.9
- weight_two: bfloat16 [384, 3, 3, 3, 384], P('rows'), may hold values from -0.0625 to 0.0625
- bias_two: float32 [384], replicated, may hold values from -3 to 3
Outputs:
- block_out: bfloat16 [64, 16, 40, 384], P('tm', 'rows')
All inputs are finite; a program needn't handle non-finite values.
Results may differ from a plain program's by a relative error of at most 0.0049.
Values may be sent and summed in bfloat16 or wider, within the bound.
No kernel may reach another device: no remote copies, remote signals or barrier semaphores. Data moves between devices by JAX's collectives and lax.ppermute only.
A program may use at most 64 MiB of HBM per device.

v0:
```python
import jax
import jax.numpy as jnp
from jax import lax
from jax.sharding import PartitionSpec as P


def passed_along(x, axis, by):
    peers = lax.axis_size(axis)
    pairs = [(i, i + by) for i in range(peers) if 0 <= i + by < peers]
    return lax.ppermute(x, axis, pairs)


def norm_silu(values, norm_gain):
    values = values.astype(jnp.float32)
    mean_square = jnp.mean(values * values, axis=-1, keepdims=True)
    scaled = values * lax.rsqrt(mean_square + 1e-06) * norm_gain
    return jax.nn.silu(scaled).astype(jnp.bfloat16)


def causal_conv(extended, kernel, bias_part):
    frames = extended.shape[0] - 2
    height = extended.shape[1]
    columns = extended.shape[2]
    channels = extended.shape[3]
    part_width = kernel.shape[0]
    folded = 9 * part_width
    padded_width = (folded + 127) // 128 * 128
    padded = jnp.pad(extended, ((0, 0), (1, 1), (1, 1), (0, 0)))
    summed = jnp.zeros((frames, height, columns, part_width), jnp.float32)
    for tap_time in range(3):
        slab = padded[tap_time : tap_time + frames]
        taps = jnp.transpose(kernel[:, tap_time], (1, 2, 0, 3)).reshape(folded, channels)
        taps = jnp.pad(taps, ((0, padded_width - folded), (0, 0)))
        product = lax.dot_general(
            slab.reshape(-1, channels),
            taps,
            (((1,), (1,)), ((), ())),
            preferred_element_type=jnp.float32,
        )
        product = product[:, :folded].reshape(frames, height + 2, columns + 2, 3, 3, part_width)
        for tap_row in range(3):
            for tap_col in range(3):
                summed = (
                    summed
                    + product[
                        :, tap_row : tap_row + height, tap_col : tap_col + columns, tap_row, tap_col
                    ]
                )
    return summed + bias_part


def shards(features, gain_one, weight_one, bias_one, gain_two, weight_two, bias_two):
    part_width = weight_one.shape[0]
    offset = lax.axis_index("rows") * part_width
    bias_first = lax.dynamic_slice_in_dim(bias_one, offset, part_width, 0)
    bias_second = lax.dynamic_slice_in_dim(bias_two, offset, part_width, 0)
    normed_one = norm_silu(features, gain_one)
    prior_one = passed_along(normed_one, "tm", 1)
    extended_one = jnp.concatenate([prior_one, normed_one], 0)
    full_one = lax.all_gather(extended_one, "rows", axis=1, tiled=True)
    conv_one = causal_conv(full_one, weight_one, bias_first).astype(jnp.bfloat16)
    own_rows = lax.all_to_all(conv_one, "rows", split_axis=1, concat_axis=3, tiled=True)
    normed_two = norm_silu(own_rows, gain_two)
    prior_two = passed_along(normed_two, "tm", 1)
    extended_two = jnp.concatenate([prior_two, normed_two], 0)
    full_two = lax.all_gather(extended_two, "rows", axis=1, tiled=True)
    conv_two = causal_conv(full_two, weight_two, bias_second)
    returned = lax.all_to_all(conv_two, "rows", split_axis=1, concat_axis=3, tiled=True)
    return (features.astype(jnp.float32) + returned).astype(jnp.bfloat16)


def solution(mesh):
    in_specs = (
        P("tm", "rows", None, None),
        P(),
        P("rows", None, None, None, None),
        P(),
        P(),
        P("rows", None, None, None, None),
        P(),
    )
    out_specs = P("tm", "rows", None, None)
    return jax.shard_map(shards, mesh=mesh, in_specs=in_specs, out_specs=out_specs, check_vma=False)
```

profile of v0, /device:TPU:1, one launch (start us, length us, event | category | flops | bytes accessed | tf_op | source)
XLA Modules:
  0.0 217.8 jit_solution(14636832090744077345)
XLA Ops:
  6.5 0.9 fusion.25
  7.5 0.9 fusion.32
  8.4 3.9 %collective-permute-start = (bf16[2,1,40,384]{3,2,1,0:T(8,128)(2,1)S(1)}, bf16[2,1,40,384]{3,2,1,0:T(8,128)(2,1)S(1)}, u32[]{:S(2)}, u32[]{:S(2)}) collective-permute-start(bf16[2,1,40,384]{3,2,1,0:T(8,128)(2,1)S(1)} %fusion.32), channel_id=1, source_target_pairs={{0,16},{16,32},{32,48},{48,64},{64,80},{80,96},{96,112},{112,128},... | collective-permute-start | bytes 184328 | tf_op jit(solution)/shard_map/ppermute | solution.py:10
  12.4 1.3 collective-permute-done
  13.7 0.7 maximum_bitcast_fusion
  14.4 0.8 dynamic_slice.6
  15.2 1.1 fusion.35
  16.3 48.9 %all-gather.3.cloned.1.call-done = bf16[4,16,40,384]{3,2,0,1:T(8,128)(2,1)} async-done(((bf16[4,1,40,384]{3,2,0,1:T(8,128)(2,1)}), bf16[4,16,40,384]{3,2,0,1:T(8,128)(2,1)}) %all-gather.3.cloned.1.call-update) | async-done | bytes 1966096 | tf_op jit(solution)/shard_map/all_gather | solution.py:60
  65.2 4.8 %pad_slice_fusion.5 = (bf16[2,18,42,384]{3,2,0,1:T(8,128)(2,1)S(1)}, bf16[2,18,42,384]{3,2,0,1:T(8,128)(2,1)}, bf16[2,18,42,384]{3,2,0,1:T(8,128)(2,1)S(1)}) fusion(bf16[4,16,40,384]{3,2,0,1:T(8,128)(2,1)} %all-gather.3.cloned.1.call-done), kind=kLoop, calls=%fused_computation.5 | loop fusion | bytes 5449728 | tf_op jit(solution)/shard_map/slice | solution.py:31
  70.2 1.3 reshape.154
  71.5 1.9 fusion.38
  73.4 4.3 %reshape.156 = f32[2,18,42,3,3,24]{2,1,0,5,4,3:T(8,128)} reshape(f32[1512,216]{0,1:T(8,128)S(1)} %fusion.38) | data formatting | bytes 2612736 | tf_op jit(solution)/shard_map/reshape | solution.py:40
  77.7 1.5 copy.58
  79.2 1.4 reshape.151
  80.5 1.9 fusion.37
  82.4 4.4 %reshape.153 = f32[2,18,42,3,3,24]{2,1,0,5,4,3:T(8,128)} reshape(f32[1512,216]{0,1:T(8,128)S(1)} %fusion.37) | data formatting | bytes 2612736 | tf_op jit(solution)/shard_map/reshape | solution.py:40
  86.9 0.3 reshape.148
  87.3 0.6 fusion.36
  87.9 4.3 %reshape.150 = f32[2,18,42,3,3,24]{2,1,0,5,4,3:T(8,128)} reshape(f32[1512,216]{0,1:T(8,128)S(1)} %fusion.36) | data formatting | bytes 2612736 | tf_op jit(solution)/shard_map/reshape | solution.py:40
  92.2 7.0 %fusion.14 = bf16[2,16,40,24]{2,1,0,3:T(8,128)(2,1)S(1)} fusion(f32[2,18,42,3,3,24]{2,1,0,5,4,3:T(8,128)} %reshape.156, f32[2,18,42,3,3,24]{2,1,0,5,4,3:T(8,128)} %reshape.153, f32[2,18,42,3,3,24]{2,1,0,5,4,3:T(8,128)} %reshape.150, f32[24]{0:T(128)S(1)} %dynamic_slice.6), kind=kLoop, calls=%fused_computation.47 | loop fusion | flops 860160 | bytes 3379296 | tf_op jit(solution)/shard_map/convert_element_type | solution.py:61
  99.3 0.2 reshape.192
  99.6 12.0 %all_to_all.27 = bf16[16,2,960]{2,1,0:T(2,128)(2,1)S(1)} all-to-all(bf16[16,2,960]{2,1,0:T(2,128)(2,1)S(1)} %reshape.192), channel_id=1, replica_groups=mesh['tm'=32,'rows'=16] {'rows'}, dimensions={0} | all-to-all | bytes 122880 | tf_op jit(solution)/shard_map/all_to_all | solution.py:62
  111.6 0.2 reshape.193
  112.0 0.4 multiply_reduce_fusion
  112.7 3.3 %collective-permute-start.1 = (bf16[2,1,40,384]{3,2,1,0:T(8,128)(2,1)S(1)}, bf16[2,1,40,384]{3,2,1,0:T(8,128)(2,1)S(1)}, u32[]{:S(2)}, u32[]{:S(2)}) collective-permute-start(bf16[2,1,40,384]{3,2,1,0:T(8,128)(2,1)S(1)} %multiply_convert_fusion), channel_id=1, source_target_pairs={{0,16},{16,32},{32,48},{48,64},{64,80},{80,96},{96,112},{112,128},... | collective-permute-start | bytes 184328 | tf_op jit(solution)/shard_map/ppermute | solution.py:10
  116.0 1.1 collective-permute-done.1
  117.1 0.7 maximum_bitcast_fusion.1
  117.8 0.8 dynamic_slice.7
  118.6 41.3 %all-gather.5.cloned.1.call-done = bf16[4,16,40,384]{3,2,0,1:T(8,128)(2,1)} async-done(((bf16[4,1,40,384]{3,2,0,1:T(8,128)(2,1)}), bf16[4,16,40,384]{3,2,0,1:T(8,128)(2,1)}) %all-gather.5.cloned.1.call-update) | async-done | bytes 1966096 | tf_op jit(solution)/shard_map/all_gather | solution.py:66
  159.9 4.8 %pad_slice_fusion.2 = (bf16[2,18,42,384]{3,2,0,1:T(8,128)(2,1)S(1)}, bf16[2,18,42,384]{3,2,0,1:T(8,128)(2,1)}, bf16[2,18,42,384]{3,2,0,1:T(8,128)(2,1)S(1)}) fusion(bf16[4,16,40,384]{3,2,0,1:T(8,128)(2,1)} %all-gather.5.cloned.1.call-done), kind=kLoop, calls=%fused_computation.2 | loop fusion | bytes 5449728 | tf_op jit(solution)/shard_map/slice | solution.py:31
  164.8 1.3 reshape.163
  166.1 1.9 fusion.41
  168.0 4.3 %reshape.165 = f32[2,18,42,3,3,24]{2,1,0,5,4,3:T(8,128)} reshape(f32[1512,216]{0,1:T(8,128)S(1)} %fusion.41) | data formatting | bytes 2612736 | tf_op jit(solution)/shard_map/reshape | solution.py:40
  172.4 1.5 copy.65
  173.8 1.4 reshape.160
  175.2 1.9 fusion.40
  177.1 4.4 %reshape.162 = f32[2,18,42,3,3,24]{2,1,0,5,4,3:T(8,128)} reshape(f32[1512,216]{0,1:T(8,128)S(1)} %fusion.40) | data formatting | bytes 2612736 | tf_op jit(solution)/shard_map/reshape | solution.py:40
  181.6 0.3 reshape.157
  181.9 0.6 fusion.39
  182.5 4.3 %reshape.159 = f32[2,18,42,3,3,24]{2,1,0,5,4,3:T(8,128)} reshape(f32[1512,216]{0,1:T(8,128)S(1)} %fusion.39) | data formatting | bytes 2612736 | tf_op jit(solution)/shard_map/reshape | solution.py:40
  186.8 7.0 %fusion.1 = f32[2,16,40,24]{2,1,0,3:T(8,128)S(1)} fusion(f32[2,18,42,3,3,24]{2,1,0,5,4,3:T(8,128)} %reshape.165, f32[2,18,42,3,3,24]{2,1,0,5,4,3:T(8,128)} %reshape.162, f32[2,18,42,3,3,24]{2,1,0,5,4,3:T(8,128)} %reshape.159, f32[24]{0:T(128)S(1)} %dynamic_slice.7), kind=kLoop, calls=%fused_computation.8 | loop fusion | flops 829440 | bytes 3440736 | tf_op jit(solution)/shard_map/add | solution.py:49
  193.8 0.2 copy.76
  194.0 0.7 reshape.194
  194.8 13.2 %all_to_all.28 = f32[16,1,1920]{2,1,0:T(1,128)S(1)} all-to-all(f32[16,1,1920]{2,1,0:T(1,128)S(1)} %reshape.194), channel_id=1, replica_groups=mesh['tm'=32,'rows'=16] {'rows'}, dimensions={0} | all-to-all | bytes 245760 | tf_op jit(solution)/shard_map/all_to_all | solution.py:68
  208.0 0.5 broadcast.93
  208.5 0.9 reduce.5
  209.4 0.7 reshape.195
  210.3 0.6 fusion.33
  (22 shorter events, 1.4 us)
Async XLA Ops:
  6.5 58.7 %all-gather.3.cloned.1.call-start = ((), (), s32[]{:S(2)}) async-start(), calls=%async_computation.2 | async-start | bytes 2088960 | tf_op jit(solution)/shard_map/all_gather | solution.py:60
  8.4 5.2 %collective-permute-start = (bf16[2,1,40,384]{3,2,1,0:T(8,128)(2,1)S(1)}, bf16[2,1,40,384]{3,2,1,0:T(8,128)(2,1)S(1)}, u32[]{:S(2)}, u32[]{:S(2)}) collective-permute-start(bf16[2,1,40,384]{3,2,1,0:T(8,128)(2,1)S(1)} %fusion.32), channel_id=1, source_target_pairs={{0,16},{16,32},{32,48},{48,64},{64,80},{80,96},{96,112},{112,128},... | collective-permute-start | bytes 184328 | tf_op jit(solution)/shard_map/ppermute | solution.py:10
  14.3 145.5 %all-gather.5.cloned.1.call-start = ((), (), s32[]{:S(2)}) async-start(), calls=%async_computation.3 | async-start | bytes 2088960 | tf_op jit(solution)/shard_map/all_gather | solution.py:66
  99.2 13.4 %copy-start.2 = (f32[384]{0:T(512)S(1)}, f32[384]{0:T(512)}, u32[]{:S(2)}) copy-start(f32[384]{0:T(512)} %param.11) | copy-start | bytes 4612
  99.3 19.2 %copy-start.1 = (bf16[24,3,3,3,384]{4,0,3,2,1:T(8,128)(2,1)S(1)}, bf16[24,3,3,3,384]{4,0,3,2,1:T(8,128)(2,1)}, u32[]{:S(2)}) copy-start(bf16[24,3,3,3,384]{4,0,3,2,1:T(8,128)(2,1)} %param.12) | copy-start | bytes 1492996
  112.7 4.4 %collective-permute-start.1 = (bf16[2,1,40,384]{3,2,1,0:T(8,128)(2,1)S(1)}, bf16[2,1,40,384]{3,2,1,0:T(8,128)(2,1)S(1)}, u32[]{:S(2)}, u32[]{:S(2)}) collective-permute-start(bf16[2,1,40,384]{3,2,1,0:T(8,128)(2,1)S(1)} %multiply_convert_fusion), channel_id=1, source_target_pairs={{0,16},{16,32},{32,48},{48,64},{64,80},{80,96},{96,112},{112,128},... | collective-permute-start | bytes 184328 | tf_op jit(solution)/shard_map/ppermute | solution.py:10
  193.8 16.5 %copy-start = (bf16[2,1,40,384]{3,2,1,0:T(8,128)(2,1)S(1)}, bf16[2,1,40,384]{3,2,1,0:T(8,128)(2,1)}, u32[]{:S(2)}) copy-start(bf16[2,1,40,384]{3,2,1,0:T(8,128)(2,1)} %param.7) | copy-start | bytes 184324
Sparse Core Ops, SparseCore 0:
  14.5 50.7 all-gather.2
  117.9 41.9 all-gather.4
where the time goes:
time: 218 us
  waiting for transfers between devices  92.6 us (42%)
  local copies, waits for them, and re-layouts  50.8 us (23%)
  blocking collectives  25.2 us (12%)
  other arithmetic  19.4 us (9%)
  between operations  13.6 us (6%)
  matrix products  8.8 us (4%)
  starting transfers between devices  7.28 us (3%)
    all_gather x1, waiting for transfers between devices, shards(): full_one = lax.all_gather(extended_one, 'rows', axis=1, tiled=True)  48.9 us
    all_gather x1, waiting for transfers between devices, shards(): full_two = lax.all_gather(extended_two, 'rows', axis=1, tiled=True)  41.3 us
    reshape x6, local copies, waits for them, and re-layouts, causal_conv(): product[:, :folded]  25.9 us
    all_to_all x1, blocking collectives, shards(): lax.all_to_all(conv_two, 'rows', split_axis=1, concat_axis=3, tiled=True)  13.2 us
    slice x8, local copies, waits for them, and re-layouts, causal_conv(): slab = padded[tap_time:tap_time + frames]  13.1 us
    all_to_all x1, blocking collectives, shards(): lax.all_to_all(conv_one, 'rows', split_axis=1, concat_axis=3, tiled=True)  12 us
    dot_general x6, matrix products, causal_conv(): lax.dot_general(slab.reshape(-1, channels), taps, (((1,), (1,)), ((), ())...  8.8 us
    ppermute x2, starting transfers between devices, passed_along(): return lax.ppermute(x, axis, pairs)  7.24 us
  transfers between devices with their start and end apart: 4, of which 4 were waited for; matrix products, arithmetic and copies ran while one was open for 1% of the time, Pallas kernels for 0%

commit v1 on v0

--- a/solution.py
+++ b/solution.py
@@ -2,6 +2,17 @@
 import jax.numpy as jnp
 from jax import lax
 from jax.sharding import PartitionSpec as P
+
+
+def pass_along(array, axis, along):
+    peers = lax.axis_size(axis)
+    route = [(i, (i + 1) % peers) for i in range(peers)]
+    parts = [array]
+    for hop in range(1, peers):
+        parts = [lax.ppermute(parts[0], axis, route), *parts]
+    full = jnp.concatenate(parts, axis=along)
+    shift = (lax.axis_index(axis) + 1) * parts[-1].shape[along]
+    return jnp.roll(full, shift, axis=along)
 
 
 def passed_along(x, axis, by):
@@ -57,7 +68,7 @@
     normed_one = norm_silu(features, gain_one)
     prior_one = passed_along(normed_one, "tm", 1)
     extended_one = jnp.concatenate([prior_one, normed_one], 0)
-    full_one = lax.all_gather(extended_one, "rows", axis=1, tiled=True)
+    full_one = pass_along(extended_one, "rows", 1)
     conv_one = causal_conv(full_one, weight_one, bias_first).astype(jnp.bfloat16)
     own_rows = lax.all_to_all(conv_one, "rows", split_axis=1, concat_axis=3, tiled=True)
     normed_two = norm_silu(own_rows, gain_two)

time: 218 us -> 263 us (1.21)
  waiting for transfers between devices: 92.6 us -> 124 us
  starting transfers between devices: 7.28 us -> 13.9 us
  blocking collectives: 25.2 us -> 31.1 us
    ppermute x0 -> x15, waiting for transfers between devices: none -> 76.6 us  [pass_along(): parts = [lax.ppermute(parts[0], axis, route), *parts]]
    all_gather x1 -> x0, waiting for transfers between devices: 48.9 us -> none  [shards(): full_one = lax.all_gather(extended_one, 'rows', axis=1, tiled=True)]
    all_to_all x1, blocking collectives: 12 us -> 17.9 us  [shards(): lax.all_to_all(conv_one, 'rows', split_axis=1, concat_axis=3, tiled=True)]
    ppermute x0 -> x15, starting transfers between devices: none -> 5.74 us  [pass_along(): parts = [lax.ppermute(parts[0], axis, route), *parts]]
    slice x8 -> x5, local copies, waits for them, and re-layouts: 13.1 us -> 8.86 us  [causal_conv(): slab = padded[tap_time:tap_time + frames]]
    all_gather x1, waiting for transfers between devices: 41.3 us -> 44.9 us  [shards(): full_two = lax.all_gather(extended_two, 'rows', axis=1, tiled=True)]
  transfers between devices with their start and end apart: 4 -> 18, of which waited for: 4 -> 18; matrix products, arithmetic and copies ran while one was open for 1% -> 1% of each run, Pallas kernels for 0% -> 0%
where the time goes in v1:
time: 263 us; the launch traced here: 262 us
  waiting for transfers between devices  124 us (47%)
  local copies, waits for them, and re-layouts  50.2 us (19%)
  blocking collectives  31.1 us (12%)
  other arithmetic  18.9 us (7%)
  starting transfers between devices  13.9 us (5%)
  between operations  13.9 us (5%)
  matrix products  10.1 us (4%)
    ppermute x15, waiting for transfers between devices, pass_along(): parts = [lax.ppermute(parts[0], axis, route), *parts]  76.6 us
    all_gather x1, waiting for transfers between devices, shards(): full_two = lax.all_gather(extended_two, 'rows', axis=1, tiled=True)  44.9 us
    reshape x6, local copies, waits for them, and re-layouts, causal_conv(): product[:, :folded]  26.1 us
    all_to_all x1, blocking collectives, shards(): lax.all_to_all(conv_one, 'rows', split_axis=1, concat_axis=3, tiled=True)  17.9 us
    all_to_all x1, blocking collectives, shards(): lax.all_to_all(conv_two, 'rows', split_axis=1, concat_axis=3, tiled=True)  13.2 us
    dot_general x6, matrix products, causal_conv(): lax.dot_general(slab.reshape(-1, channels), taps, (((1,), (1,)), ((), ())...  10.1 us
    slice x5, local copies, waits for them, and re-layouts, causal_conv(): slab = padded[tap_time:tap_time + frames]  8.86 us
    reshape x6, local copies, waits for them, and re-layouts, causal_conv(): slab.reshape(-1, channels)  8.65 us
  transfers between devices with their start and end apart: 18, of which 18 were waited for; matrix products, arithmetic and copies ran while one was open for 1% of the time, Pallas kernels for 0%

profile of v1, /device:TPU:1, one launch (start us, length us, event | category | flops | bytes accessed | tf_op | source)
XLA Modules:
  0.0 261.9 jit_solution(17799050292261665568)
XLA Ops:
  7.5 0.9 fusion.32
  8.4 3.9 %collective-permute-start = (bf16[2,1,40,384]{3,2,1,0:T(8,128)(2,1)S(1)}, bf16[2,1,40,384]{3,2,1,0:T(8,128)(2,1)S(1)}, u32[]{:S(2)}, u32[]{:S(2)}) collective-permute-start(bf16[2,1,40,384]{3,2,1,0:T(8,128)(2,1)S(1)} %fusion.32), channel_id=1, source_target_pairs={{0,16},{16,32},{32,48},{48,64},{64,80},{80,96},{96,112},{112,128},... | collective-permute-start | bytes 184328 | tf_op jit(solution)/shard_map/ppermute | solution.py:21
  12.4 1.3 collective-permute-done
  13.7 3.5 %collective-permute-start.1 = (bf16[4,1,40,384]{3,2,1,0:T(8,128)(2,1)S(1)}, bf16[4,1,40,384]{3,2,1,0:T(8,128)(2,1)S(1)}, u32[]{:S(2)}, u32[]{:S(2)}) collective-permute-start(bf16[4,1,40,384]{3,2,1,0:T(8,128)(2,1)S(1)} %pad_maximum_fusion), channel_id=1, source_target_pairs={{0,1},{1,2},{2,3},{3,4},{4,5},{5,6},{6,7},{7,8},{8,9},{9,10},{10,1... | collective-permute-start | bytes 368648 | tf_op jit(solution)/shard_map/ppermute | solution.py:12
  17.2 2.1 collective-permute-done.1
  19.3 2.2 collective-permute-start.2
  21.5 4.7 %collective-permute-done.2 = bf16[4,1,40,384]{3,2,1,0:T(8,128)(2,1)S(1)} collective-permute-done((bf16[4,1,40,384]{3,2,1,0:T(8,128)(2,1)S(1)}, bf16[4,1,40,384]{3,2,1,0:T(8,128)(2,1)S(1)}, u32[]{:S(2)}, u32[]{:S(2)}) %collective-permute-start.2) | collective-permute-done | bytes 122912 | tf_op jit(solution)/shard_map/ppermute | solution.py:12
  26.2 5.5 %collective-permute-done.3 = bf16[4,1,40,384]{3,2,1,0:T(8,128)(2,1)S(1)} collective-permute-done((bf16[4,1,40,384]{3,2,1,0:T(8,128)(2,1)S(1)}, bf16[4,1,40,384]{3,2,1,0:T(8,128)(2,1)S(1)}, u32[]{:S(2)}, u32[]{:S(2)}) %collective-permute-start.3) | collective-permute-done | bytes 122912 | tf_op jit(solution)/shard_map/ppermute | solution.py:12
  31.8 5.5 %collective-permute-done.4 = bf16[4,1,40,384]{3,2,1,0:T(8,128)(2,1)S(1)} collective-permute-done((bf16[4,1,40,384]{3,2,1,0:T(8,128)(2,1)S(1)}, bf16[4,1,40,384]{3,2,1,0:T(8,128)(2,1)S(1)}, u32[]{:S(2)}, u32[]{:S(2)}) %collective-permute-start.4) | collective-permute-done | bytes 122912 | tf_op jit(solution)/shard_map/ppermute | solution.py:12
  37.3 5.5 %collective-permute-done.5 = bf16[4,1,40,384]{3,2,1,0:T(8,128)(2,1)S(1)} collective-permute-done((bf16[4,1,40,384]{3,2,1,0:T(8,128)(2,1)S(1)}, bf16[4,1,40,384]{3,2,1,0:T(8,128)(2,1)S(1)}, u32[]{:S(2)}, u32[]{:S(2)}) %collective-permute-start.5) | collective-permute-done | bytes 122912 | tf_op jit(solution)/shard_map/ppermute | solution.py:12
  42.8 5.5 %collective-permute-done.6 = bf16[4,1,40,384]{3,2,1,0:T(8,128)(2,1)S(1)} collective-permute-done((bf16[4,1,40,384]{3,2,1,0:T(8,128)(2,1)S(1)}, bf16[4,1,40,384]{3,2,1,0:T(8,128)(2,1)S(1)}, u32[]{:S(2)}, u32[]{:S(2)}) %collective-permute-start.6) | collective-permute-done | bytes 122912 | tf_op jit(solution)/shard_map/ppermute | solution.py:12
  48.3 5.5 %collective-permute-done.7 = bf16[4,1,40,384]{3,2,1,0:T(8,128)(2,1)S(1)} collective-permute-done((bf16[4,1,40,384]{3,2,1,0:T(8,128)(2,1)S(1)}, bf16[4,1,40,384]{3,2,1,0:T(8,128)(2,1)S(1)}, u32[]{:S(2)}, u32[]{:S(2)}) %collective-permute-start.7) | collective-permute-done | bytes 122912 | tf_op jit(solution)/shard_map/ppermute | solution.py:12
  53.8 5.5 %collective-permute-done.8 = bf16[4,1,40,384]{3,2,1,0:T(8,128)(2,1)S(1)} collective-permute-done((bf16[4,1,40,384]{3,2,1,0:T(8,128)(2,1)S(1)}, bf16[4,1,40,384]{3,2,1,0:T(8,128)(2,1)S(1)}, u32[]{:S(2)}, u32[]{:S(2)}) %collective-permute-start.8) | collective-permute-done | bytes 122912 | tf_op jit(solution)/shard_map/ppermute | solution.py:12
  59.3 5.5 %collective-permute-done.9 = bf16[4,1,40,384]{3,2,1,0:T(8,128)(2,1)S(1)} collective-permute-done((bf16[4,1,40,384]{3,2,1,0:T(8,128)(2,1)S(1)}, bf16[4,1,40,384]{3,2,1,0:T(8,128)(2,1)S(1)}, u32[]{:S(2)}, u32[]{:S(2)}) %collective-permute-start.9) | collective-permute-done | bytes 122912 | tf_op jit(solution)/shard_map/ppermute | solution.py:12
  64.9 5.5 %collective-permute-done.10 = bf16[4,1,40,384]{3,2,1,0:T(8,128)(2,1)S(1)} collective-permute-done((bf16[4,1,40,384]{3,2,1,0:T(8,128)(2,1)S(1)}, bf16[4,1,40,384]{3,2,1,0:T(8,128)(2,1)S(1)}, u32[]{:S(2)}, u32[]{:S(2)}) %collective-permute-start.10) | collective-permute-done | bytes 122912 | tf_op jit(solution)/shard_map/ppermute | solution.py:12
  70.4 5.5 %collective-permute-done.11 = bf16[4,1,40,384]{3,2,1,0:T(8,128)(2,1)S(1)} collective-permute-done((bf16[4,1,40,384]{3,2,1,0:T(8,128)(2,1)S(1)}, bf16[4,1,40,384]{3,2,1,0:T(8,128)(2,1)S(1)}, u32[]{:S(2)}, u32[]{:S(2)}) %collective-permute-start.11) | collective-permute-done | bytes 122912 | tf_op jit(solution)/shard_map/ppermute | solution.py:12
  75.9 5.5 %collective-permute-done.12 = bf16[4,1,40,384]{3,2,1,0:T(8,128)(2,1)S(1)} collective-permute-done((bf16[4,1,40,384]{3,2,1,0:T(8,128)(2,1)S(1)}, bf16[4,1,40,384]{3,2,1,0:T(8,128)(2,1)S(1)}, u32[]{:S(2)}, u32[]{:S(2)}) %collective-permute-start.12) | collective-permute-done | bytes 122912 | tf_op jit(solution)/shard_map/ppermute | solution.py:12
  81.4 5.5 %collective-permute-done.13 = bf16[4,1,40,384]{3,2,1,0:T(8,128)(2,1)S(1)} collective-permute-done((bf16[4,1,40,384]{3,2,1,0:T(8,128)(2,1)S(1)}, bf16[4,1,40,384]{3,2,1,0:T(8,128)(2,1)S(1)}, u32[]{:S(2)}, u32[]{:S(2)}) %collective-permute-start.13) | collective-permute-done | bytes 122912 | tf_op jit(solution)/shard_map/ppermute | solution.py:12
  87.7 4.8 %collective-permute-done.14 = bf16[4,1,40,384]{3,2,1,0:T(8,128)(2,1)S(1)} collective-permute-done((bf16[4,1,40,384]{3,2,1,0:T(8,128)(2,1)S(1)}, bf16[4,1,40,384]{3,2,1,0:T(8,128)(2,1)S(1)}, u32[]{:S(2)}, u32[]{:S(2)}) %collective-permute-start.14) | collective-permute-done | bytes 122912 | tf_op jit(solution)/shard_map/ppermute | solution.py:12
  92.4 1.1 fusion.35
  93.6 4.4 %collective-permute-done.15 = bf16[4,1,40,384]{3,2,1,0:T(8,128)(2,1)S(1)} collective-permute-done((bf16[4,1,40,384]{3,2,1,0:T(8,128)(2,1)S(1)}, bf16[4,1,40,384]{3,2,1,0:T(8,128)(2,1)S(1)}, u32[]{:S(2)}, u32[]{:S(2)}) %collective-permute-start.15) | collective-permute-done | bytes 122912 | tf_op jit(solution)/shard_map/ppermute | solution.py:12
  99.1 2.3 pad_slice_fusion.5
  101.4 1.4 reshape.148
  102.8 1.9 fusion.36
  104.7 4.4 %reshape.150 = f32[2,18,42,3,3,24]{2,1,0,5,4,3:T(8,128)} reshape(f32[1512,216]{0,1:T(8,128)S(1)} %fusion.36) | data formatting | bytes 2612736 | tf_op jit(solution)/shard_map/reshape | solution.py:51
  109.0 2.9 %reshape.151 = bf16[1512,384]{1,0:T(8,128)(2,1)} reshape(bf16[2,18,42,384]{3,2,1,0:T(8,128)(2,1)} %get-tuple-element.9) | data formatting | bytes 2322432 | tf_op jit(solution)/shard_map/reshape | solution.py:46
  112.0 1.9 fusion.37
  113.9 4.3 %reshape.153 = f32[2,18,42,3,3,24]{2,1,0,5,4,3:T(8,128)} reshape(f32[1512,216]{0,1:T(8,128)S(1)} %fusion.37) | data formatting | bytes 2612736 | tf_op jit(solution)/shard_map/reshape | solution.py:51
  118.2 1.3 reshape.154
  119.5 1.9 fusion.38
  121.4 4.3 %reshape.156 = f32[2,18,42,3,3,24]{2,1,0,5,4,3:T(8,128)} reshape(f32[1512,216]{0,1:T(8,128)S(1)} %fusion.38) | data formatting | bytes 2612736 | tf_op jit(solution)/shard_map/reshape | solution.py:51
  125.8 7.0 %fusion.14 = bf16[2,16,40,24]{2,1,0,3:T(8,128)(2,1)S(1)} fusion(f32[2,18,42,3,3,24]{2,1,0,5,4,3:T(8,128)} %reshape.156, f32[2,18,42,3,3,24]{2,1,0,5,4,3:T(8,128)} %reshape.153, f32[2,18,42,3,3,24]{2,1,0,5,4,3:T(8,128)} %reshape.150, f32[24]{0:T(128)S(1)} %dynamic_slice.11), kind=kLoop, calls=%fused_computation.47 | loop fusion | flops 860160 | bytes 3379296 | tf_op jit(solution)/shard_map/convert_element_type | solution.py:72
  133.2 17.9 %all_to_all.27 = bf16[16,2,960]{2,1,0:T(2,128)(2,1)S(1)} all-to-all(bf16[16,2,960]{2,1,0:T(2,128)(2,1)S(1)} %reshape.192), channel_id=1, replica_groups=mesh['tm'=32,'rows'=16] {'rows'}, dimensions={0} | all-to-all | bytes 122880 | tf_op jit(solution)/shard_map/all_to_all | solution.py:73
  152.2 4.2 %collective-permute-start.16 = (bf16[2,1,40,384]{3,2,1,0:T(8,128)(2,1)S(1)}, bf16[2,1,40,384]{3,2,1,0:T(8,128)(2,1)S(1)}, u32[]{:S(2)}, u32[]{:S(2)}) collective-permute-start(bf16[2,1,40,384]{3,2,1,0:T(8,128)(2,1)S(1)} %multiply_convert_fusion), channel_id=1, source_target_pairs={{0,16},{16,32},{32,48},{48,64},{64,80},{80,96},{96,112},{112,128},... | collective-permute-start | bytes 184328 | tf_op jit(solution)/shard_map/ppermute | solution.py:21
  156.4 1.1 collective-permute-done.16
  159.0 44.9 %all-gather.2.cloned.1.call-done = bf16[4,16,40,384]{3,2,0,1:T(8,128)(2,1)} async-done(((bf16[4,1,40,384]{3,2,0,1:T(8,128)(2,1)}), bf16[4,16,40,384]{3,2,0,1:T(8,128)(2,1)}) %all-gather.2.cloned.1.call-update) | async-done | bytes 1966096 | tf_op jit(solution)/shard_map/all_gather | solution.py:77
  203.9 4.8 %pad_slice_fusion.2 = (bf16[2,18,42,384]{3,2,0,1:T(8,128)(2,1)S(1)}, bf16[2,18,42,384]{3,2,0,1:T(8,128)(2,1)}, bf16[2,18,42,384]{3,2,0,1:T(8,128)(2,1)S(1)}) fusion(bf16[4,16,40,384]{3,2,0,1:T(8,128)(2,1)} %all-gather.2.cloned.1.call-done), kind=kLoop, calls=%fused_computation.2 | loop fusion | bytes 5449728 | tf_op jit(solution)/shard_map/slice | solution.py:42
  208.9 1.4 reshape.157
  210.2 1.9 fusion.39
  212.1 4.4 %reshape.159 = f32[2,18,42,3,3,24]{2,1,0,5,4,3:T(8,128)} reshape(f32[1512,216]{0,1:T(8,128)S(1)} %fusion.39) | data formatting | bytes 2612736 | tf_op jit(solution)/shard_map/reshape | solution.py:51
  216.5 1.5 copy.55
  217.9 1.4 reshape.160
  219.3 1.9 fusion.40
  221.2 4.3 %reshape.162 = f32[2,18,42,3,3,24]{2,1,0,5,4,3:T(8,128)} reshape(f32[1512,216]{0,1:T(8,128)S(1)} %fusion.40) | data formatting | bytes 2612736 | tf_op jit(solution)/shard_map/reshape | solution.py:51
  226.6 4.3 %reshape.165 = f32[2,18,42,3,3,24]{2,1,0,5,4,3:T(8,128)} reshape(f32[1512,216]{0,1:T(8,128)S(1)} %fusion.41) | data formatting | bytes 2612736 | tf_op jit(solution)/shard_map/reshape | solution.py:51
  231.0 7.0 %fusion.1 = f32[2,16,40,24]{2,1,0,3:T(8,128)S(1)} fusion(f32[2,18,42,3,3,24]{2,1,0,5,4,3:T(8,128)} %reshape.165, f32[2,18,42,3,3,24]{2,1,0,5,4,3:T(8,128)} %reshape.162, f32[2,18,42,3,3,24]{2,1,0,5,4,3:T(8,128)} %reshape.159, f32[24]{0:T(128)S(1)} %dynamic_slice.12), kind=kLoop, calls=%fused_computation.8 | loop fusion | flops 829440 | bytes 3440736 | tf_op jit(solution)/shard_map/add | solution.py:60
  238.9 13.2 %all_to_all.28 = f32[16,1,1920]{2,1,0:T(1,128)S(1)} all-to-all(f32[16,1,1920]{2,1,0:T(1,128)S(1)} %reshape.194), channel_id=1, replica_groups=mesh['tm'=32,'rows'=16] {'rows'}, dimensions={0} | all-to-all | bytes 245760 | tf_op jit(solution)/shard_map/all_to_all | solution.py:79
  252.6 0.9 reduce.5
  (79 shorter events, 9.7 us)
Async XLA Ops:
  6.5 197.4 %all-gather.2.cloned.1.call-start = ((), (), s32[]{:S(2)}) async-start(), calls=%async_computation.2 | async-start | bytes 2088960 | tf_op jit(solution)/shard_map/all_gather | solution.py:77
  8.4 5.2 %collective-permute-start = (bf16[2,1,40,384]{3,2,1,0:T(8,128)(2,1)S(1)}, bf16[2,1,40,384]{3,2,1,0:T(8,128)(2,1)S(1)}, u32[]{:S(2)}, u32[]{:S(2)}) collective-permute-start(bf16[2,1,40,384]{3,2,1,0:T(8,128)(2,1)S(1)} %fusion.32), channel_id=1, source_target_pairs={{0,16},{16,32},{32,48},{48,64},{64,80},{80,96},{96,112},{112,128},... | collective-permute-start | bytes 184328 | tf_op jit(solution)/shard_map/ppermute | solution.py:21
  13.7 5.6 %collective-permute-start.1 = (bf16[4,1,40,384]{3,2,1,0:T(8,128)(2,1)S(1)}, bf16[4,1,40,384]{3,2,1,0:T(8,128)(2,1)S(1)}, u32[]{:S(2)}, u32[]{:S(2)}) collective-permute-start(bf16[4,1,40,384]{3,2,1,0:T(8,128)(2,1)S(1)} %pad_maximum_fusion), channel_id=1, source_target_pairs={{0,1},{1,2},{2,3},{3,4},{4,5},{5,6},{6,7},{7,8},{8,9},{9,10},{10,1... | collective-permute-start | bytes 368648 | tf_op jit(solution)/shard_map/ppermute | solution.py:12
  19.3 6.9 %collective-permute-start.2 = (bf16[4,1,40,384]{3,2,1,0:T(8,128)(2,1)S(1)}, bf16[4,1,40,384]{3,2,1,0:T(8,128)(2,1)S(1)}, u32[]{:S(2)}, u32[]{:S(2)}) collective-permute-start(bf16[4,1,40,384]{3,2,1,0:T(8,128)(2,1)S(1)} %collective-permute-done.1), channel_id=1, source_target_pairs={{0,1},{1,2},{2,3},{3,4},{4,5},{5,6},{6,7},{7,8},{8,9},{9,10},{10,1... | collective-permute-start | bytes 368648 | tf_op jit(solution)/shard_map/ppermute | solution.py:12
  26.2 5.5 %collective-permute-start.3 = (bf16[4,1,40,384]{3,2,1,0:T(8,128)(2,1)S(1)}, bf16[4,1,40,384]{3,2,1,0:T(8,128)(2,1)S(1)}, u32[]{:S(2)}, u32[]{:S(2)}) collective-permute-start(bf16[4,1,40,384]{3,2,1,0:T(8,128)(2,1)S(1)} %collective-permute-done.2), channel_id=1, source_target_pairs={{0,1},{1,2},{2,3},{3,4},{4,5},{5,6},{6,7},{7,8},{8,9},{9,10},{10,1... | collective-permute-start | bytes 368648 | tf_op jit(solution)/shard_map/ppermute | solution.py:12
  31.8 5.5 %collective-permute-start.4 = (bf16[4,1,40,384]{3,2,1,0:T(8,128)(2,1)S(1)}, bf16[4,1,40,384]{3,2,1,0:T(8,128)(2,1)S(1)}, u32[]{:S(2)}, u32[]{:S(2)}) collective-permute-start(bf16[4,1,40,384]{3,2,1,0:T(8,128)(2,1)S(1)} %collective-permute-done.3), channel_id=1, source_target_pairs={{0,1},{1,2},{2,3},{3,4},{4,5},{5,6},{6,7},{7,8},{8,9},{9,10},{10,1... | collective-permute-start | bytes 368648 | tf_op jit(solution)/shard_map/ppermute | solution.py:12
  37.3 5.5 %collective-permute-start.5 = (bf16[4,1,40,384]{3,2,1,0:T(8,128)(2,1)S(1)}, bf16[4,1,40,384]{3,2,1,0:T(8,128)(2,1)S(1)}, u32[]{:S(2)}, u32[]{:S(2)}) collective-permute-start(bf16[4,1,40,384]{3,2,1,0:T(8,128)(2,1)S(1)} %collective-permute-done.4), channel_id=1, source_target_pairs={{0,1},{1,2},{2,3},{3,4},{4,5},{5,6},{6,7},{7,8},{8,9},{9,10},{10,1... | collective-permute-start | bytes 368648 | tf_op jit(solution)/shard_map/ppermute | solution.py:12
  42.8 5.5 %collective-permute-start.6 = (bf16[4,1,40,384]{3,2,1,0:T(8,128)(2,1)S(1)}, bf16[4,1,40,384]{3,2,1,0:T(8,128)(2,1)S(1)}, u32[]{:S(2)}, u32[]{:S(2)}) collective-permute-start(bf16[4,1,40,384]{3,2,1,0:T(8,128)(2,1)S(1)} %collective-permute-done.5), channel_id=1, source_target_pairs={{0,1},{1,2},{2,3},{3,4},{4,5},{5,6},{6,7},{7,8},{8,9},{9,10},{10,1... | collective-permute-start | bytes 368648 | tf_op jit(solution)/shard_map/ppermute | solution.py:12
  48.3 5.5 %collective-permute-start.7 = (bf16[4,1,40,384]{3,2,1,0:T(8,128)(2,1)S(1)}, bf16[4,1,40,384]{3,2,1,0:T(8,128)(2,1)S(1)}, u32[]{:S(2)}, u32[]{:S(2)}) collective-permute-start(bf16[4,1,40,384]{3,2,1,0:T(8,128)(2,1)S(1)} %collective-permute-done.6), channel_id=1, source_target_pairs={{0,1},{1,2},{2,3},{3,4},{4,5},{5,6},{6,7},{7,8},{8,9},{9,10},{10,1... | collective-permute-start | bytes 368648 | tf_op jit(solution)/shard_map/ppermute | solution.py:12
  53.8 5.5 %collective-permute-start.8 = (bf16[4,1,40,384]{3,2,1,0:T(8,128)(2,1)S(1)}, bf16[4,1,40,384]{3,2,1,0:T(8,128)(2,1)S(1)}, u32[]{:S(2)}, u32[]{:S(2)}) collective-permute-start(bf16[4,1,40,384]{3,2,1,0:T(8,128)(2,1)S(1)} %collective-permute-done.7), channel_id=1, source_target_pairs={{0,1},{1,2},{2,3},{3,4},{4,5},{5,6},{6,7},{7,8},{8,9},{9,10},{10,1... | collective-permute-start | bytes 368648 | tf_op jit(solution)/shard_map/ppermute | solution.py:12
  59.3 5.5 %collective-permute-start.9 = (bf16[4,1,40,384]{3,2,1,0:T(8,128)(2,1)S(1)}, bf16[4,1,40,384]{3,2,1,0:T(8,128)(2,1)S(1)}, u32[]{:S(2)}, u32[]{:S(2)}) collective-permute-start(bf16[4,1,40,384]{3,2,1,0:T(8,128)(2,1)S(1)} %collective-permute-done.8), channel_id=1, source_target_pairs={{0,1},{1,2},{2,3},{3,4},{4,5},{5,6},{6,7},{7,8},{8,9},{9,10},{10,1... | collective-permute-start | bytes 368648 | tf_op jit(solution)/shard_map/ppermute | solution.py:12
  64.9 5.5 %collective-permute-start.10 = (bf16[4,1,40,384]{3,2,1,0:T(8,128)(2,1)S(1)}, bf16[4,1,40,384]{3,2,1,0:T(8,128)(2,1)S(1)}, u32[]{:S(2)}, u32[]{:S(2)}) collective-permute-start(bf16[4,1,40,384]{3,2,1,0:T(8,128)(2,1)S(1)} %collective-permute-done.9), channel_id=1, source_target_pairs={{0,1},{1,2},{2,3},{3,4},{4,5},{5,6},{6,7},{7,8},{8,9},{9,10},{10,1... | collective-permute-start | bytes 368648 | tf_op jit(solution)/shard_map/ppermute | solution.py:12
  70.4 5.5 %collective-permute-start.11 = (bf16[4,1,40,384]{3,2,1,0:T(8,128)(2,1)S(1)}, bf16[4,1,40,384]{3,2,1,0:T(8,128)(2,1)S(1)}, u32[]{:S(2)}, u32[]{:S(2)}) collective-permute-start(bf16[4,1,40,384]{3,2,1,0:T(8,128)(2,1)S(1)} %collective-permute-done.10), channel_id=1, source_target_pairs={{0,1},{1,2},{2,3},{3,4},{4,5},{5,6},{6,7},{7,8},{8,9},{9,10},{10,1... | collective-permute-start | bytes 368648 | tf_op jit(solution)/shard_map/ppermute | solution.py:12
  75.9 5.5 %collective-permute-start.12 = (bf16[4,1,40,384]{3,2,1,0:T(8,128)(2,1)S(1)}, bf16[4,1,40,384]{3,2,1,0:T(8,128)(2,1)S(1)}, u32[]{:S(2)}, u32[]{:S(2)}) collective-permute-start(bf16[4,1,40,384]{3,2,1,0:T(8,128)(2,1)S(1)} %collective-permute-done.11), channel_id=1, source_target_pairs={{0,1},{1,2},{2,3},{3,4},{4,5},{5,6},{6,7},{7,8},{8,9},{9,10},{10,1... | collective-permute-start | bytes 368648 | tf_op jit(solution)/shard_map/ppermute | solution.py:12
  81.4 5.5 %collective-permute-start.13 = (bf16[4,1,40,384]{3,2,1,0:T(8,128)(2,1)S(1)}, bf16[4,1,40,384]{3,2,1,0:T(8,128)(2,1)S(1)}, u32[]{:S(2)}, u32[]{:S(2)}) collective-permute-start(bf16[4,1,40,384]{3,2,1,0:T(8,128)(2,1)S(1)} %collective-permute-done.12), channel_id=1, source_target_pairs={{0,1},{1,2},{2,3},{3,4},{4,5},{5,6},{6,7},{7,8},{8,9},{9,10},{10,1... | collective-permute-start | bytes 368648 | tf_op jit(solution)/shard_map/ppermute | solution.py:12
  86.9 5.5 %collective-permute-start.14 = (bf16[4,1,40,384]{3,2,1,0:T(8,128)(2,1)S(1)}, bf16[4,1,40,384]{3,2,1,0:T(8,128)(2,1)S(1)}, u32[]{:S(2)}, u32[]{:S(2)}) collective-permute-start(bf16[4,1,40,384]{3,2,1,0:T(8,128)(2,1)S(1)} %collective-permute-done.13), channel_id=1, source_target_pairs={{0,1},{1,2},{2,3},{3,4},{4,5},{5,6},{6,7},{7,8},{8,9},{9,10},{10,1... | collective-permute-start | bytes 368648 | tf_op jit(solution)/shard_map/ppermute | solution.py:12
  92.4 5.5 %collective-permute-start.15 = (bf16[4,1,40,384]{3,2,1,0:T(8,128)(2,1)S(1)}, bf16[4,1,40,384]{3,2,1,0:T(8,128)(2,1)S(1)}, u32[]{:S(2)}, u32[]{:S(2)}) collective-permute-start(bf16[4,1,40,384]{3,2,1,0:T(8,128)(2,1)S(1)} %collective-permute-done.14), channel_id=1, source_target_pairs={{0,1},{1,2},{2,3},{3,4},{4,5},{5,6},{6,7},{7,8},{8,9},{9,10},{10,1... | collective-permute-start | bytes 368648 | tf_op jit(solution)/shard_map/ppermute | solution.py:12
  125.8 26.3 %copy-start.2 = (f32[384]{0:T(512)S(1)}, f32[384]{0:T(512)}, u32[]{:S(2)}) copy-start(f32[384]{0:T(512)} %param.11) | copy-start | bytes 4612
  125.8 33.1 %copy-start.1 = (bf16[24,3,3,3,384]{4,0,3,2,1:T(8,128)(2,1)S(1)}, bf16[24,3,3,3,384]{4,0,3,2,1:T(8,128)(2,1)}, u32[]{:S(2)}) copy-start(bf16[24,3,3,3,384]{4,0,3,2,1:T(8,128)(2,1)} %param.12) | copy-start | bytes 1492996
  152.2 5.3 %collective-permute-start.16 = (bf16[2,1,40,384]{3,2,1,0:T(8,128)(2,1)S(1)}, bf16[2,1,40,384]{3,2,1,0:T(8,128)(2,1)S(1)}, u32[]{:S(2)}, u32[]{:S(2)}) collective-permute-start(bf16[2,1,40,384]{3,2,1,0:T(8,128)(2,1)S(1)} %multiply_convert_fusion), channel_id=1, source_target_pairs={{0,16},{16,32},{32,48},{48,64},{64,80},{80,96},{96,112},{112,128},... | collective-permute-start | bytes 184328 | tf_op jit(solution)/shard_map/ppermute | solution.py:21
  231.0 23.5 %copy-start = (bf16[2,1,40,384]{3,2,1,0:T(8,128)(2,1)S(1)}, bf16[2,1,40,384]{3,2,1,0:T(8,128)(2,1)}, u32[]{:S(2)}) copy-start(bf16[2,1,40,384]{3,2,1,0:T(8,128)(2,1)} %param.7) | copy-start | bytes 184324
Sparse Core Ops, SparseCore 0:
  158.3 45.5 all-gather.1
